TPU v7x, 256 devices: a whole 4x4x8 slice. The times are simulated.
256 devices in a mesh: gx: 64 (over z, y, core), gy: 4 (over x).
Axes of the slice: x: 4, y: 4, z: 8, core: 2. Of those that a mesh axis runs over, the one named last changes fastest.
Arguments:
- embeds: bfloat16 [256, 2048, 768], P('gx', 'gy'), may hold values from -6 to 6
- fetch_list: int32 [2, 64, 64], replicated, may hold values from 0 to 16383, as said below
- partners: int32 [2, 64, 64, 2], replicated, may hold values from 0 to 255, as said below
- counts: int32 [256], replicated, may hold values from 512 to 2048
Outputs:
- nearest: float32 [256, 2048], P('gx', 'gy')
Inputs may be any that keep to these rules, and one draw needn't show every extreme that they name: fetch_list[w, h, g] // 64 is a block stored by index g of gx, that is g * 4 <= fetch_list[w, h, g] // 64 < (g + 1) * 4. partners[w, h, g, :] are 2 different blocks stored by index h of gx, none equal to fetch_list[w, h, g] // 64.
All inputs are finite; a program needn't handle non-finite values.
Results may differ from a plain program's by a relative error of at most 0.0003.
Values may be sent and summed in bfloat16 or wider, within the bound.
No kernel may reach another device: no remote copies, remote signals or barrier semaphores. Data moves between devices by JAX's collectives and lax.ppermute only.
A program may use at most 192 MiB of HBM per device.

v0:
```python
import jax
import jax.numpy as jnp
from jax import lax
from jax.sharding import PartitionSpec as P

SLICE = 8
EPS = 1e-06


def normalize(source):
    values = source.astype(jnp.float32)
    return (values * lax.rsqrt(jnp.sum(values * values, axis=-1, keepdims=True) + EPS)).astype(
        jnp.bfloat16
    )


def dense_tiles(arrived, row_valid, chosen, owned_full, col_valid):
    slots, lent_rows, width = arrived.shape
    owned, block, _ = owned_full.shape
    flat_rows = arrived.reshape(slots * lent_rows, width)
    listed = jnp.any(
        chosen[:, :, None] == jnp.arange(owned, dtype=jnp.int32)[None, None, :], axis=1
    )
    listed_pairs = jnp.transpose(listed.reshape(slots, owned // 2, 2), (1, 0, 2))
    column_pairs = owned_full.reshape(owned // 2, 2, block, width)
    valid_pairs = col_valid.reshape(owned // 2, 2, block)

    def advance(best_rows, entries):
        columns, picked, valid_cols = entries
        scores = jnp.einsum("rd,cbd->rcb", flat_rows, columns, preferred_element_type=jnp.float32)
        scores = scores.reshape(slots, lent_rows, 2, block)
        keep = row_valid[:, :, None, None] & picked[:, None, :, None] & valid_cols[None, None, :, :]
        scores = jnp.where(keep, scores, jnp.float32(-1.0))
        return (jnp.maximum(best_rows, jnp.max(scores, axis=(2, 3))), jnp.max(scores, axis=(0, 1)))

    start = jnp.full((slots, lent_rows), -1.0, jnp.float32)
    best_rows, col_parts = lax.scan(advance, start, (column_pairs, listed_pairs, valid_pairs))
    return (best_rows, col_parts.reshape(owned, block))


def on_device(embeds, fetch_list, partners, counts):
    owned, quarter, width = embeds.shape
    slice_rows = SLICE
    pieces = quarter // slice_rows
    my_group = lax.axis_index("gx")
    my_lane = lax.axis_index("gy")
    block = quarter * lax.axis_size("gy")
    first = my_group * owned
    waves = fetch_list.shape[0]
    own_unit = normalize(embeds)
    own_pieces = own_unit.reshape(owned, pieces, slice_rows, width)
    owned_full = lax.all_gather(own_unit, "gy", axis=1, tiled=True)
    positions = jnp.arange(block, dtype=jnp.int32)
    own_counts = lax.dynamic_slice_in_dim(counts, first, owned)
    col_valid = positions[None, :] < own_counts[:, None]
    row_positions = my_lane * quarter + jnp.arange(quarter, dtype=jnp.int32)
    slice_offsets = my_lane * quarter + jnp.arange(slice_rows, dtype=jnp.int32)
    local_ids = jnp.arange(owned, dtype=jnp.int32)
    piece_ids = jnp.arange(pieces, dtype=jnp.int32)
    row_total = jnp.full((owned, quarter), -1.0, jnp.float32)
    col_total = jnp.full((owned, block), -1.0, jnp.float32)
    for wave_index in range(waves):
        tiles = lax.dynamic_index_in_dim(fetch_list[wave_index], my_group, 1, False)
        outgoing_sent_block = tiles // pieces - first
        outgoing_sent_piece = tiles % pieces
        outbound = own_pieces[outgoing_sent_block, outgoing_sent_piece]
        arrived = lax.all_to_all(outbound, "gx", split_axis=0, concat_axis=0, tiled=True)
        incoming = lax.dynamic_index_in_dim(fetch_list[wave_index], my_group, 0, False)
        arrived_counts = counts[incoming // pieces]
        arrived_rows = (incoming % pieces)[:, None] * slice_rows + slice_offsets[None, :]
        row_valid = arrived_rows < arrived_counts[:, None]
        chosen = lax.dynamic_index_in_dim(partners[wave_index], my_group, 0, False) - first
        row_best, col_best = dense_tiles(arrived, row_valid, chosen, owned_full, col_valid)
        returned = lax.all_to_all(row_best, "gx", split_axis=0, concat_axis=0, tiled=True)
        match = (outgoing_sent_block[:, None, None] == local_ids[None, :, None]) & (
            outgoing_sent_piece[:, None, None] == piece_ids[None, None, :]
        )
        placed = jnp.max(
            jnp.where(match[:, :, :, None], returned[:, None, None, :], jnp.float32(-1.0)), axis=0
        )
        row_total = jnp.maximum(row_total, placed.reshape(owned, quarter))
        col_total = jnp.maximum(col_total, col_best)
    col_all = lax.pmax(col_total, "gy")
    col_mine = lax.dynamic_slice_in_dim(col_all, my_lane * quarter, quarter, 1)
    nearest = jnp.maximum(row_total, col_mine)
    mine_valid = row_positions[None, :] < own_counts[:, None]
    return jnp.where(mine_valid, nearest, jnp.float32(-1.0))


def solution(mesh):
    in_specs = (P("gx", "gy", None), P(), P(), P())
    out_specs = P("gx", "gy")
    return jax.shard_map(
        on_device, mesh=mesh, in_specs=in_specs, out_specs=out_specs, check_vma=False
    )
```

profile of v0, /device:TPU:1, one launch (start us, length us, event | category | flops | bytes accessed | tf_op | source)
XLA Modules:
  0.0 224.2 jit_solution(3750707437659595756)
XLA Ops:
  6.5 2.7 %fusion.18 = f32[4,512]{1,0:T(4,128)S(1)} fusion(bf16[4,512,768]{2,1,0:T(8,128)(2,1)} %param.8), kind=kLoop, calls=%fused_computation.36 | loop fusion | flops 4716544 | bytes 3153920 | tf_op jit(solution)/shard_map/reduce_sum | solution.py:12
  9.3 4.1 %fusion.19 = bf16[4,512,768]{2,1,0:T(8,128)(2,1)} fusion(bf16[4,512,768]{2,1,0:T(8,128)(2,1)} %param.8, f32[4,512]{1,0:T(4,128)S(1)} %add_rsqrt_fusion), kind=kLoop, calls=%fused_computation.37 | loop fusion | flops 4718592 | bytes 6299648 | tf_op jit(solution)/shard_map/convert_element_type | solution.py:12
  13.4 0.0 all-gather.2.cloned.1.call-update
  13.5 0.2 dynamic-slice_reduce_fusion
  13.7 2.2 %fusion.48 = bf16[4,64,8,768]{3,2,1,0:T(8,128)(2,1)} fusion(f32[4,512]{1,0:T(4,128)S(1)} %add_rsqrt_fusion, bf16[4,512,768]{2,1,0:T(8,128)(2,1)S(1)} %copy-done.1), kind=kLoop, calls=%fused_computation.135 | loop fusion | flops 4718592 | bytes 6299648 | tf_op jit(solution)/shard_map/reshape | solution.py:51
  16.0 3.5 %gather_fusion.3 = bf16[64,8,768]{2,1,0:T(8,128)(2,1)} fusion(bf16[4,64,8,768]{3,2,1,0:T(8,128)(2,1)} %fusion.48, s32[64]{0:T(128)S(1)} %fusion.42), kind=kCustom, calls=%fused_computation.3 | custom fusion | bytes 1573376 | tf_op jit(solution)/shard_map/gather | solution.py:66
  19.4 13.1 %all-to-all-start.2 = ((bf16[64,8,768]{2,1,0:T(8,128)(2,1)}), bf16[64,8,768]{2,1,0:T(8,128)(2,1)S(1)}, u32[]{:S(2)}, u32[]{:S(2)}) async-start(bf16[64,8,768]{2,1,0:T(8,128)(2,1)} %gather_fusion.3), calls=%async_computation.2 | async-start | bytes 1572864 | tf_op jit(solution)/shard_map/all_to_all | solution.py:67
  32.7 0.1 dynamic_slice.48
  32.8 0.1 lt.161
  32.9 0.8 gather_fusion.2
  33.7 0.2 dynamic-slice_reduce_fusion.1
  33.9 3.7 %gather_fusion.1 = bf16[64,8,768]{2,1,0:T(8,128)(2,1)} fusion(bf16[4,64,8,768]{3,2,1,0:T(8,128)(2,1)} %fusion.48, s32[64]{0:T(128)S(1)} %fusion.43), kind=kCustom, calls=%fused_computation.1 | custom fusion | bytes 1573376 | tf_op jit(solution)/shard_map/gather | solution.py:66
  37.7 0.8 gather_fusion
  38.5 0.1 iota_compare_fusion
  38.6 0.1 iota_compare_fusion.1
  38.7 0.1 iota_compare_fusion.3
  38.8 0.1 iota_compare_fusion.4
  38.8 0.1 broadcast_and_fusion.2
  39.0 0.1 broadcast_and_fusion.3
  39.1 0.1 iota_compare_fusion.2
  39.2 16.4 %all-to-all-done.2 = bf16[64,8,768]{2,1,0:T(8,128)(2,1)S(1)} async-done(((bf16[64,8,768]{2,1,0:T(8,128)(2,1)}), bf16[64,8,768]{2,1,0:T(8,128)(2,1)S(1)}, u32[]{:S(2)}, u32[]{:S(2)}) %all-to-all-start.2) | async-done | bytes 786464 | tf_op jit(solution)/shard_map/all_to_all | solution.py:67
  55.6 5.9 %all-to-all-start = ((bf16[64,8,768]{2,1,0:T(8,128)(2,1)}), bf16[64,8,768]{2,1,0:T(8,128)(2,1)S(1)}, u32[]{:S(2)}, u32[]{:S(2)}) async-start(bf16[64,8,768]{2,1,0:T(8,128)(2,1)} %gather_fusion.1), calls=%async_computation | async-start | bytes 1572864 | tf_op jit(solution)/shard_map/all_to_all | solution.py:67
  61.5 76.8 %all-gather.2.cloned.1.call-done = bf16[4,2048,768]{2,1,0:T(8,128)(2,1)} async-done(((bf16[4,512,768]{2,1,0:T(8,128)(2,1)}), bf16[4,2048,768]{2,1,0:T(8,128)(2,1)}) %all-gather.2.cloned.1.call-update) | async-done | bytes 12582928 | tf_op jit(solution)/shard_map/all_gather | solution.py:52
  138.3 15.5 %while.27 = (s32[]{:T(128)}, f32[64,8]{1,0:T(8,128)}, f32[2,2,2048]{2,1,0:T(2,128)S(1)}, pred[2,64,2]{1,2,0:T(4,128)(4,1)S(1)}, pred[2,2,2048]{2,1,0:T(4,128)(4,...) while((s32[]{:T(128)}, f32[64,8]{1,0:T(8,128)}, ...), condition=%wide.region_11.12_spmd.clone, body=%wide.region_8.11_spmd.clone.sunk | while | flops 3229612544 | bytes 7160887 | solution.py:37
  138.4 0.1 and.439
  138.5 0.1 and.440
  138.6 0.1 add_compare_fusion.5
  138.7 0.1 and.441
  138.8 6.2 %fusion.52 = (f32[2,2048]{1,0:T(2,128)S(1)}, f32[512]{0:T(512)S(1)}) fusion(pred[2,2048]{1,0:T(4,128)(4,1)S(1)} %dynamic-slice_bitcast_fusion.10, pred[512,2]{0,1:T(4,128)(4,1)S(1)} %broadcast_and_fusion.7, bf16[512,768]{1,0:T(8,128)(2,1)S(1)} %get-tuple-element.389, bf16[2,2,2048,768]{3,2,1,0:T(8,128)(2,1)} %get-tuple-element.388, s32[]{:T(128)S(6)} %copy.19), kind=kOutput, calls=%fused_computation.21.clone.1 | convolution fusion | flops 3229609472 | bytes 7101444 | tf_op jit(solution)/shard_map/while/body/eval_jaxpr/rd,cbd->rcb/dot_general | solution.py:30
  145.0 0.1 reduce_max.79
  145.1 0.6 select_maximum_fusion.5
  145.8 0.1 and.439
  145.9 0.1 and.440
  146.0 0.1 add_compare_fusion.5
  146.1 0.1 and.441
  146.2 6.2 %fusion.52 = (f32[2,2048]{1,0:T(2,128)S(1)}, f32[512]{0:T(512)S(1)}) fusion(pred[2,2048]{1,0:T(4,128)(4,1)S(1)} %dynamic-slice_bitcast_fusion.10, pred[512,2]{0,1:T(4,128)(4,1)S(1)} %broadcast_and_fusion.7, bf16[512,768]{1,0:T(8,128)(2,1)S(1)} %get-tuple-element.389, bf16[2,2,2048,768]{3,2,1,0:T(8,128)(2,1)} %get-tuple-element.388, s32[]{:T(128)S(6)} %copy.19), kind=kOutput, calls=%fused_computation.21.clone.1 | convolution fusion | flops 3229609472 | bytes 7101444 | tf_op jit(solution)/shard_map/while/body/eval_jaxpr/rd,cbd->rcb/dot_general | solution.py:30
  152.4 0.1 reduce_max.79
  152.5 1.4 select_maximum_fusion.5
  153.9 0.0 all-to-all-done
  153.9 10.9 %all-to-all-start.3 = ((f32[64,1,8]{2,1,0:T(1,128)}), f32[64,1,8]{2,1,0:T(1,128)S(1)}, u32[]{:S(2)}, u32[]{:S(2)}) async-start(f32[64,1,8]{2,1,0:T(1,128)} %bitcast.18), calls=%async_computation.3 | async-start | bytes 65536 | tf_op jit(solution)/shard_map/all_to_all | solution.py:74
  164.8 15.5 %while.26 = (s32[]{:T(128)}, f32[64,8]{1,0:T(8,128)}, f32[2,2,2048]{2,1,0:T(2,128)S(1)}, pred[2,64,2]{1,2,0:T(4,128)(4,1)S(1)}, pred[2,2,2048]{2,1,0:T(4,128)(4,...) while((s32[]{:T(128)}, f32[64,8]{1,0:T(8,128)}, ...), condition=%wide.region_5.6_spmd.clone, body=%wide.region_2.5_spmd.clone.sunk | while | flops 3229612544 | bytes 7160887 | solution.py:37
  164.8 0.1 and.431
  164.9 0.1 and.432
  165.0 0.1 add_compare_fusion.4
  165.1 0.1 and.433
  165.2 6.2 %fusion.51 = (f32[2,2048]{1,0:T(2,128)S(1)}, f32[512]{0:T(512)S(1)}) fusion(pred[2,2048]{1,0:T(4,128)(4,1)S(1)} %dynamic-slice_bitcast_fusion.8, pred[512,2]{0,1:T(4,128)(4,1)S(1)} %broadcast_and_fusion.6, bf16[512,768]{1,0:T(8,128)(2,1)S(1)} %get-tuple-element.425, bf16[2,2,2048,768]{3,2,1,0:T(8,128)(2,1)} %get-tuple-element.424, s32[]{:T(128)S(6)} %copy.28), kind=kOutput, calls=%fused_computation.7.clone.1 | convolution fusion | flops 3229609472 | bytes 7101444 | tf_op jit(solution)/shard_map/while/body/eval_jaxpr/rd,cbd->rcb/dot_general | solution.py:30
  171.4 0.1 reduce_max.77
  171.5 0.6 select_maximum_fusion.4
  172.2 0.1 and.431
  172.3 0.1 and.432
  172.4 0.1 add_compare_fusion.4
  172.5 0.1 and.433
  172.6 6.2 %fusion.51 = (f32[2,2048]{1,0:T(2,128)S(1)}, f32[512]{0:T(512)S(1)}) fusion(pred[2,2048]{1,0:T(4,128)(4,1)S(1)} %dynamic-slice_bitcast_fusion.8, pred[512,2]{0,1:T(4,128)(4,1)S(1)} %broadcast_and_fusion.6, bf16[512,768]{1,0:T(8,128)(2,1)S(1)} %get-tuple-element.425, bf16[2,2,2048,768]{3,2,1,0:T(8,128)(2,1)} %get-tuple-element.424, s32[]{:T(128)S(6)} %copy.28), kind=kOutput, calls=%fused_computation.7.clone.1 | convolution fusion | flops 3229609472 | bytes 7101444 | tf_op jit(solution)/shard_map/while/body/eval_jaxpr/rd,cbd->rcb/dot_general | solution.py:30
  178.8 0.1 reduce_max.77
  178.9 1.4 select_maximum_fusion.4
  180.4 12.3 %pmax.7 = f32[4,2048]{1,0:T(4,128)S(1)} all-reduce(f32[4,2048]{1,0:T(4,128)S(1)} %max.26), channel_id=1, replica_groups=mesh['gx'=64,'gy'=4] {'gy'}, use_global_device_ids=true, to_apply=%region_13.14 | all-reduce | flops 8192 | bytes 65536 | tf_op jit(solution)/shard_map/pmax | solution.py:83
  192.7 0.0 all-to-all-done.3
  192.7 14.1 %all-to-all-start.1 = ((f32[64,1,8]{2,1,0:T(1,128)}), f32[64,1,8]{2,1,0:T(1,128)S(1)}, u32[]{:S(2)}, u32[]{:S(2)}) async-start(f32[64,1,8]{2,1,0:T(1,128)} %bitcast.9), calls=%async_computation.1 | async-start | bytes 65536 | tf_op jit(solution)/shard_map/all_to_all | solution.py:74
  206.8 0.2 select_reduce_fusion
  207.0 9.2 %all-to-all-done.1 = f32[64,1,8]{2,1,0:T(1,128)S(1)} async-done(((f32[64,1,8]{2,1,0:T(1,128)}), f32[64,1,8]{2,1,0:T(1,128)S(1)}, u32[]{:S(2)}, u32[]{:S(2)}) %all-to-all-start.1) | async-done | bytes 2080 | tf_op jit(solution)/shard_map/all_to_all | solution.py:74
  216.2 0.2 select_reduce_fusion.1
  216.4 0.1 copy.13
  216.5 0.1 max.24
  216.6 0.7 maximum_select_fusion
  (50 shorter events, 0.5 us)
Async XLA Ops:
  6.5 7.2 %copy-start.1 = (bf16[4,512,768]{2,1,0:T(8,128)(2,1)S(1)}, bf16[4,512,768]{2,1,0:T(8,128)(2,1)}, u32[]{:S(2)}) copy-start(bf16[4,512,768]{2,1,0:T(8,128)(2,1)} %param.8) | copy-start | bytes 9437188
  6.5 6.9 %copy-start.3 = (s32[2,64,64]{2,1,0:T(8,128)S(1)}, s32[2,64,64]{2,1,0:T(8,128)}, u32[]{:S(2)}) copy-start(s32[2,64,64]{2,1,0:T(8,128)} %param.9) | copy-start | bytes 98308
  6.5 131.8 %all-gather.2.cloned.1.call-start = ((), (), s32[]{:S(2)}) async-start(), calls=%async_computation.4 | async-start | bytes 15728640 | tf_op jit(solution)/shard_map/all_gather | solution.py:52
  13.4 19.2 %copy-start.2 = (s32[2,64,64,2]{2,3,1,0:T(2,128)S(1)}, s32[2,64,64,2]{2,3,1,0:T(2,128)}, u32[]{:S(2)}) copy-start(s32[2,64,64,2]{2,3,1,0:T(2,128)} %param.10) | copy-start | bytes 196612
  13.4 19.2 %copy-start = (s32[256]{0:T(256)S(1)}, s32[256]{0:T(256)}, u32[]{:S(2)}) copy-start(s32[256]{0:T(256)} %param.11) | copy-start | bytes 3076
  19.4 36.2 %all-to-all-start.2 = ((bf16[64,8,768]{2,1,0:T(8,128)(2,1)}), bf16[64,8,768]{2,1,0:T(8,128)(2,1)S(1)}, u32[]{:S(2)}, u32[]{:S(2)}) async-start(bf16[64,8,768]{2,1,0:T(8,128)(2,1)} %gather_fusion.3), calls=%async_computation.2 | async-start | bytes 1572864 | tf_op jit(solution)/shard_map/all_to_all | solution.py:67
  55.6 98.3 %all-to-all-start = ((bf16[64,8,768]{2,1,0:T(8,128)(2,1)}), bf16[64,8,768]{2,1,0:T(8,128)(2,1)S(1)}, u32[]{:S(2)}, u32[]{:S(2)}) async-start(bf16[64,8,768]{2,1,0:T(8,128)(2,1)} %gather_fusion.1), calls=%async_computation | async-start | bytes 1572864 | tf_op jit(solution)/shard_map/all_to_all | solution.py:67
  153.9 38.8 %all-to-all-start.3 = ((f32[64,1,8]{2,1,0:T(1,128)}), f32[64,1,8]{2,1,0:T(1,128)S(1)}, u32[]{:S(2)}, u32[]{:S(2)}) async-start(f32[64,1,8]{2,1,0:T(1,128)} %bitcast.18), calls=%async_computation.3 | async-start | bytes 65536 | tf_op jit(solution)/shard_map/all_to_all | solution.py:74
  192.7 23.5 %all-to-all-start.1 = ((f32[64,1,8]{2,1,0:T(1,128)}), f32[64,1,8]{2,1,0:T(1,128)S(1)}, u32[]{:S(2)}, u32[]{:S(2)}) async-start(f32[64,1,8]{2,1,0:T(1,128)} %bitcast.9), calls=%async_computation.1 | async-start | bytes 65536 | tf_op jit(solution)/shard_map/all_to_all | solution.py:74
Sparse Core Ops, SparseCore 0:
  13.6 124.6 all-gather.1
where the time goes:
time: 225 us; the launch traced here: 224 us
  waiting for transfers between devices  102 us (45%)
  starting transfers between devices  44 us (20%)
  matrix products  24.8 us (11%)
  other arithmetic  15.5 us (7%)
  between operations  13.7 us (6%)
  blocking collectives  12.3 us (5%)
  local copies, waits for them, and re-layouts  11.2 us (5%)
    all_gather x1, waiting for transfers between devices, on_device(): owned_full = lax.all_gather(own_unit, 'gy', axis=1, tiled=True)  76.8 us
    all_to_all x2, starting transfers between devices, on_device(): lax.all_to_all(row_best, 'gx', split_axis=0, concat_axis=0, tiled=True)  24.9 us
    dot_general x4, matrix products, advance(): jnp.einsum('rd,cbd->rcb', flat_rows, columns, preferred_element_type=jnp....  24.8 us
    all_to_all x2, starting transfers between devices, on_device(): lax.all_to_all(outbound, 'gx', split_axis=0, concat_axis=0, tiled=True)  19.1 us
    all_to_all x2, waiting for transfers between devices, on_device(): lax.all_to_all(outbound, 'gx', split_axis=0, concat_axis=0, tiled=True)  16.4 us
    pmax x1, blocking collectives, on_device(): col_all = lax.pmax(col_total, 'gy')  12.3 us
    all_to_all x2, waiting for transfers between devices, on_device(): lax.all_to_all(row_best, 'gx', split_axis=0, concat_axis=0, tiled=True)  9.17 us
    gather x2, local copies, waits for them, and re-layouts, on_device(): outbound = own_pieces[outgoing_sent_block, outgoing_sent_piece]  7.19 us
  transfers between devices with their start and end apart: 5, of which 3 were waited for; matrix products, arithmetic and copies ran while one was open for 19% of the time, Pallas kernels for 0%

commit v1 on v0

--- a/solution.py
+++ b/solution.py
@@ -1,3 +1,4 @@
+import functools
 import jax
 import jax.numpy as jnp
 from jax import lax
@@ -5,6 +6,16 @@
 
 SLICE = 8
 EPS = 1e-06
+
+
+def register_sheet_in(slab_in, named_axis):
+    buffer = []
+    for _ in range(lax.psum(1, named_axis)):
+        buffer.append(slab_in)
+    return jnp.concatenate(lax.all_to_all(jnp.stack(buffer, axis=0), named_axis, 0, 0), axis=1)
+
+
+move_stops_all = functools.partial(register_sheet_in, named_axis="gy")
 
 
 def normalize(source):
@@ -49,7 +60,7 @@
     waves = fetch_list.shape[0]
     own_unit = normalize(embeds)
     own_pieces = own_unit.reshape(owned, pieces, slice_rows, width)
-    owned_full = lax.all_gather(own_unit, "gy", axis=1, tiled=True)
+    owned_full = move_stops_all(own_unit)
     positions = jnp.arange(block, dtype=jnp.int32)
     own_counts = lax.dynamic_slice_in_dim(counts, first, owned)
     col_valid = positions[None, :] < own_counts[:, None]

time: 225 us -> 280 us (1.24)
  waiting for transfers between devices: 102 us -> 153 us
  local copies, waits for them, and re-layouts: 11.2 us -> 27.5 us
  between operations: 13.7 us -> 0.29 us
  starting transfers between devices: 44 us -> 47.8 us
    all_to_all x0 -> x1, waiting for transfers between devices: none -> 125 us  [register_sheet_in(): lax.all_to_all(jnp.stack(buffer, axis=0), named_axis, 0, 0)]
    all_gather x1 -> x0, waiting for transfers between devices: 76.8 us -> none  [on_device(): owned_full = lax.all_gather(own_unit, 'gy', axis=1, tiled=True)]
    all_to_all x0 -> x1, local copies, waits for them, and re-layouts: none -> 10.7 us  [register_sheet_in(): lax.all_to_all(jnp.stack(buffer, axis=0), named_axis, 0, 0)]
    all_to_all x0 -> x1, starting transfers between devices: none -> 6.61 us  [register_sheet_in(): lax.all_to_all(jnp.stack(buffer, axis=0), named_axis, 0, 0)]
    another operation x2 -> x3, local copies, waits for them, and re-layouts: 0.02 us -> 5.81 us  [the longest x1 5.79 us: register_sheet_in(): jnp.stack(buffer, axis=0)]
    all_to_all x2, starting transfers between devices: 24.9 us -> 19.9 us  [on_device(): lax.all_to_all(row_best, 'gx', split_axis=0, concat_axis=0, tiled=True)]
  transfers between devices with their start and end apart: 5 -> 5, of which waited for: 3 -> 4; matrix products, arithmetic and copies ran while one was open for 19% -> 19% of each run, Pallas kernels for 0% -> 0%
where the time goes in v1:
time: 280 us; the launch traced here: 279 us
  waiting for transfers between devices  153 us (55%)
  starting transfers between devices  47.8 us (17%)
  local copies, waits for them, and re-layouts  27.5 us (10%)
  matrix products  24.9 us (9%)
  other arithmetic  13.7 us (5%)
  blocking collectives  11.8 us (4%)
    all_to_all x1, waiting for transfers between devices, register_sheet_in(): lax.all_to_all(jnp.stack(buffer, axis=0), named_axis, 0, 0)  125 us
    dot_general x4, matrix products, advance(): jnp.einsum('rd,cbd->rcb', flat_rows, columns, preferred_element_type=jnp....  24.9 us
    all_to_all x2, starting transfers between devices, on_device(): lax.all_to_all(outbound, 'gx', split_axis=0, concat_axis=0, tiled=True)  21.2 us
    all_to_all x2, starting transfers between devices, on_device(): lax.all_to_all(row_best, 'gx', split_axis=0, concat_axis=0, tiled=True)  19.9 us
    all_to_all x2, waiting for transfers between devices, on_device(): lax.all_to_all(outbound, 'gx', split_axis=0, concat_axis=0, tiled=True)  19.2 us
    pmax x1, blocking collectives, on_device(): col_all = lax.pmax(col_total, 'gy')  11.8 us
    all_to_all x1, local copies, waits for them, and re-layouts, register_sheet_in(): lax.all_to_all(jnp.stack(buffer, axis=0), named_axis, 0, 0)  10.7 us
    all_to_all x2, waiting for transfers between devices, on_device(): lax.all_to_all(row_best, 'gx', split_axis=0, concat_axis=0, tiled=True)  9.18 us
  transfers between devices with their start and end apart: 5, of which 4 were waited for; matrix products, arithmetic and copies ran while one was open for 19% of the time, Pallas kernels for 0%

profile of v1, /device:TPU:1, one launch (start us, length us, event | category | flops | bytes accessed | tf_op | source)
XLA Modules:
  0.0 279.5 jit_solution(2758956721859116921)
XLA Ops:
  0.0 2.6 fusion.18
  2.6 2.5 fusion.19
  5.1 5.8 %stack.2 = bf16[4,4,512,768]{3,2,1,0:T(8,128)(2,1)} broadcast(bf16[4,512,768]{2,1,0:T(8,128)(2,1)S(1)} %fusion.19), dimensions={1,2,3} | broadcast | bytes 15728640 | tf_op jit(solution)/shard_map/stack | solution.py:15
  10.9 6.6 %all-to-all-start = ((bf16[4,4,512,768]{3,2,1,0:T(8,128)(2,1)}), bf16[4,4,512,768]{3,2,1,0:T(8,128)(2,1)}, u32[]{:S(2)}, u32[]{:S(2)}) async-start(bf16[4,4,512,768]{3,2,1,0:T(8,128)(2,1)} %stack.2), calls=%async_computation | async-start | bytes 25165824 | tf_op jit(solution)/shard_map/all_to_all | solution.py:15
  17.6 0.1 dynamic_slice.48
  17.7 0.1 lt.161
  17.8 0.8 gather_fusion.2
  18.7 0.2 dynamic-slice_reduce_fusion
  18.9 2.3 fusion.48
  21.2 3.5 %gather_fusion.3 = bf16[64,8,768]{2,1,0:T(8,128)(2,1)} fusion(bf16[4,64,8,768]{3,2,1,0:T(8,128)(2,1)} %fusion.48, s32[64]{0:T(128)S(1)} %fusion.42), kind=kCustom, calls=%fused_computation.3 | custom fusion | bytes 1573376 | tf_op jit(solution)/shard_map/gather | solution.py:77
  24.7 0.2 dynamic-slice_reduce_fusion.1
  24.9 3.5 %gather_fusion.1 = bf16[64,8,768]{2,1,0:T(8,128)(2,1)} fusion(bf16[4,64,8,768]{3,2,1,0:T(8,128)(2,1)} %fusion.48, s32[64]{0:T(128)S(1)} %fusion.43), kind=kCustom, calls=%fused_computation.1 | custom fusion | bytes 1573376 | tf_op jit(solution)/shard_map/gather | solution.py:77
  28.4 0.8 gather_fusion
  29.3 0.1 iota_compare_fusion
  29.3 125.0 %all-to-all-done = bf16[4,4,512,768]{3,2,1,0:T(8,128)(2,1)} async-done(((bf16[4,4,512,768]{3,2,1,0:T(8,128)(2,1)}), bf16[4,4,512,768]{3,2,1,0:T(8,128)(2,1)}, u32[]{:S(2)}, u32[]{:S(2)}) %all-to-all-start) | async-done | bytes 12582944 | tf_op jit(solution)/shard_map/all_to_all | solution.py:15
  154.4 15.3 %all-to-all-start.3 = ((bf16[64,8,768]{2,1,0:T(8,128)(2,1)}), bf16[64,8,768]{2,1,0:T(8,128)(2,1)S(1)}, u32[]{:S(2)}, u32[]{:S(2)}) async-start(bf16[64,8,768]{2,1,0:T(8,128)(2,1)} %gather_fusion.3), calls=%async_computation.3 | async-start | bytes 1572864 | tf_op jit(solution)/shard_map/all_to_all | solution.py:78
  169.7 0.1 iota_compare_fusion.1
  169.8 0.1 iota_compare_fusion.4
  169.9 0.1 broadcast_and_fusion.2
  170.0 0.1 broadcast_and_fusion.3
  170.2 0.1 iota_compare_fusion.2
  170.3 10.7 %copy.16 = bf16[4,4,512,768]{3,2,0,1:T(8,128)(2,1)} copy(bf16[4,4,512,768]{3,2,1,0:T(8,128)(2,1)} %all-to-all-done) | data formatting | bytes 25165824 | tf_op jit(solution)/shard_map/all_to_all | solution.py:15
  181.0 11.7 %all-to-all-done.3 = bf16[64,8,768]{2,1,0:T(8,128)(2,1)S(1)} async-done(((bf16[64,8,768]{2,1,0:T(8,128)(2,1)}), bf16[64,8,768]{2,1,0:T(8,128)(2,1)S(1)}, u32[]{:S(2)}, u32[]{:S(2)}) %all-to-all-start.3) | async-done | bytes 786464 | tf_op jit(solution)/shard_map/all_to_all | solution.py:78
  192.7 5.9 %all-to-all-start.1 = ((bf16[64,8,768]{2,1,0:T(8,128)(2,1)}), bf16[64,8,768]{2,1,0:T(8,128)(2,1)S(1)}, u32[]{:S(2)}, u32[]{:S(2)}) async-start(bf16[64,8,768]{2,1,0:T(8,128)(2,1)} %gather_fusion.1), calls=%async_computation.1 | async-start | bytes 1572864 | tf_op jit(solution)/shard_map/all_to_all | solution.py:78
  198.6 15.5 %while.27 = (s32[]{:T(128)}, f32[64,8]{1,0:T(8,128)}, f32[2,2,2048]{2,1,0:T(2,128)S(1)}, pred[2,64,2]{1,2,0:T(4,128)(4,1)S(1)}, pred[2,2,2048]{2,1,0:T(4,128)(4,...) while((s32[]{:T(128)}, f32[64,8]{1,0:T(8,128)}, ...), condition=%wide.region_11.12_spmd.clone, body=%wide.region_8.11_spmd.clone.sunk | while | flops 3229612544 | bytes 7160887 | solution.py:48
  198.7 0.1 and.439
  198.7 0.1 and.440
  198.9 0.1 add_compare_fusion.5
  198.9 0.1 and.441
  199.1 6.2 %fusion.52 = (f32[2,2048]{1,0:T(2,128)S(1)}, f32[512]{0:T(512)S(1)}) fusion(pred[2,2048]{1,0:T(4,128)(4,1)S(1)} %dynamic-slice_bitcast_fusion.10, pred[512,2]{0,1:T(4,128)(4,1)S(1)} %broadcast_and_fusion.7, bf16[512,768]{1,0:T(8,128)(2,1)S(1)} %get-tuple-element.389, bf16[2,2,2048,768]{3,2,1,0:T(8,128)(2,1)} %get-tuple-element.388, s32[]{:T(128)S(6)} %copy.23), kind=kOutput, calls=%fused_computation.21.clone.1 | convolution fusion | flops 3229609472 | bytes 7101444 | tf_op jit(solution)/shard_map/while/body/eval_jaxpr/rd,cbd->rcb/dot_general | solution.py:41
  205.3 0.1 reduce_max.79
  205.4 0.6 select_maximum_fusion.5
  206.0 0.1 and.439
  206.1 0.1 and.440
  206.2 0.1 add_compare_fusion.5
  206.3 0.1 and.441
  206.4 6.2 %fusion.52 = (f32[2,2048]{1,0:T(2,128)S(1)}, f32[512]{0:T(512)S(1)}) fusion(pred[2,2048]{1,0:T(4,128)(4,1)S(1)} %dynamic-slice_bitcast_fusion.10, pred[512,2]{0,1:T(4,128)(4,1)S(1)} %broadcast_and_fusion.7, bf16[512,768]{1,0:T(8,128)(2,1)S(1)} %get-tuple-element.389, bf16[2,2,2048,768]{3,2,1,0:T(8,128)(2,1)} %get-tuple-element.388, s32[]{:T(128)S(6)} %copy.23), kind=kOutput, calls=%fused_computation.21.clone.1 | convolution fusion | flops 3229609472 | bytes 7101444 | tf_op jit(solution)/shard_map/while/body/eval_jaxpr/rd,cbd->rcb/dot_general | solution.py:41
  212.7 0.1 reduce_max.79
  212.8 1.4 select_maximum_fusion.5
  214.1 7.4 %all-to-all-done.1 = bf16[64,8,768]{2,1,0:T(8,128)(2,1)S(1)} async-done(((bf16[64,8,768]{2,1,0:T(8,128)(2,1)}), bf16[64,8,768]{2,1,0:T(8,128)(2,1)S(1)}, u32[]{:S(2)}, u32[]{:S(2)}) %all-to-all-start.1) | async-done | bytes 786464 | tf_op jit(solution)/shard_map/all_to_all | solution.py:78
  221.6 5.9 %all-to-all-start.4 = ((f32[64,1,8]{2,1,0:T(1,128)}), f32[64,1,8]{2,1,0:T(1,128)S(1)}, u32[]{:S(2)}, u32[]{:S(2)}) async-start(f32[64,1,8]{2,1,0:T(1,128)} %bitcast.20), calls=%async_computation.4 | async-start | bytes 65536 | tf_op jit(solution)/shard_map/all_to_all | solution.py:85
  227.5 15.5 %while.26 = (s32[]{:T(128)}, f32[64,8]{1,0:T(8,128)}, f32[2,2,2048]{2,1,0:T(2,128)S(1)}, pred[2,64,2]{1,2,0:T(4,128)(4,1)S(1)}, pred[2,2,2048]{2,1,0:T(4,128)(4,...) while((s32[]{:T(128)}, f32[64,8]{1,0:T(8,128)}, ...), condition=%wide.region_5.6_spmd.clone, body=%wide.region_2.5_spmd.clone.sunk | while | flops 3229612544 | bytes 7160887 | solution.py:48
  227.6 0.1 and.431
  227.7 0.1 and.432
  227.8 0.1 add_compare_fusion.4
  227.9 0.1 and.433
  228.0 6.2 %fusion.51 = (f32[2,2048]{1,0:T(2,128)S(1)}, f32[512]{0:T(512)S(1)}) fusion(pred[2,2048]{1,0:T(4,128)(4,1)S(1)} %dynamic-slice_bitcast_fusion.8, pred[512,2]{0,1:T(4,128)(4,1)S(1)} %broadcast_and_fusion.6, bf16[512,768]{1,0:T(8,128)(2,1)S(1)} %get-tuple-element.425, bf16[2,2,2048,768]{3,2,1,0:T(8,128)(2,1)} %get-tuple-element.424, s32[]{:T(128)S(6)} %copy.32), kind=kOutput, calls=%fused_computation.7.clone.1 | convolution fusion | flops 3229609472 | bytes 7101444 | tf_op jit(solution)/shard_map/while/body/eval_jaxpr/rd,cbd->rcb/dot_general | solution.py:41
  234.2 0.1 reduce_max.77
  234.3 0.6 select_maximum_fusion.4
  235.0 0.1 and.431
  235.0 0.1 and.432
  235.2 0.1 add_compare_fusion.4
  235.2 0.1 and.433
  235.4 6.2 %fusion.51 = (f32[2,2048]{1,0:T(2,128)S(1)}, f32[512]{0:T(512)S(1)}) fusion(pred[2,2048]{1,0:T(4,128)(4,1)S(1)} %dynamic-slice_bitcast_fusion.8, pred[512,2]{0,1:T(4,128)(4,1)S(1)} %broadcast_and_fusion.6, bf16[512,768]{1,0:T(8,128)(2,1)S(1)} %get-tuple-element.425, bf16[2,2,2048,768]{3,2,1,0:T(8,128)(2,1)} %get-tuple-element.424, s32[]{:T(128)S(6)} %copy.32), kind=kOutput, calls=%fused_computation.7.clone.1 | convolution fusion | flops 3229609472 | bytes 7101444 | tf_op jit(solution)/shard_map/while/body/eval_jaxpr/rd,cbd->rcb/dot_general | solution.py:41
  241.6 0.1 reduce_max.77
  241.7 1.4 select_maximum_fusion.4
  243.1 11.8 %pmax.7 = f32[4,2048]{1,0:T(4,128)S(1)} all-reduce(f32[4,2048]{1,0:T(4,128)S(1)} %max.26), channel_id=1, replica_groups=mesh['gx'=64,'gy'=4] {'gy'}, use_global_device_ids=true, to_apply=%region_13.14 | all-reduce | flops 8192 | bytes 65536 | tf_op jit(solution)/shard_map/pmax | solution.py:94
  254.9 14.0 %all-to-all-start.2 = ((f32[64,1,8]{2,1,0:T(1,128)}), f32[64,1,8]{2,1,0:T(1,128)S(1)}, u32[]{:S(2)}, u32[]{:S(2)}) async-start(f32[64,1,8]{2,1,0:T(1,128)} %bitcast.10), calls=%async_computation.2 | async-start | bytes 65536 | tf_op jit(solution)/shard_map/all_to_all | solution.py:85
  268.9 0.2 select_reduce_fusion
  269.2 9.2 %all-to-all-done.2 = f32[64,1,8]{2,1,0:T(1,128)S(1)} async-done(((f32[64,1,8]{2,1,0:T(1,128)}), f32[64,1,8]{2,1,0:T(1,128)S(1)}, u32[]{:S(2)}, u32[]{:S(2)}) %all-to-all-start.2) | async-done | bytes 2080 | tf_op jit(solution)/shard_map/all_to_all | solution.py:85
  278.3 0.2 select_reduce_fusion.1
  278.6 0.1 copy.17
  278.7 0.1 max.24
  278.8 0.7 maximum_select_fusion
  (51 shorter events, 0.6 us)
Async XLA Ops:
  10.9 6.7 %copy-start.2 = (s32[2,64,64,2]{2,3,1,0:T(2,128)S(1)}, s32[2,64,64,2]{2,3,1,0:T(2,128)}, u32[]{:S(2)}) copy-start(s32[2,64,64,2]{2,3,1,0:T(2,128)} %param.10) | copy-start | bytes 196612
  10.9 6.7 %copy-start = (s32[256]{0:T(256)S(1)}, s32[256]{0:T(256)}, u32[]{:S(2)}) copy-start(s32[256]{0:T(256)} %param.11) | copy-start | bytes 3076
  10.9 6.9 %copy-start.3 = (s32[2,64,64]{2,1,0:T(8,128)S(1)}, s32[2,64,64]{2,1,0:T(8,128)}, u32[]{:S(2)}) copy-start(s32[2,64,64]{2,1,0:T(8,128)} %param.9) | copy-start | bytes 98308
  10.9 8.0 %copy-start.1 = (bf16[4,512,768]{2,1,0:T(8,128)(2,1)S(1)}, bf16[4,512,768]{2,1,0:T(8,128)(2,1)}, u32[]{:S(2)}) copy-start(bf16[4,512,768]{2,1,0:T(8,128)(2,1)} %param.8) | copy-start | bytes 9437188
  10.9 143.5 %all-to-all-start = ((bf16[4,4,512,768]{3,2,1,0:T(8,128)(2,1)}), bf16[4,4,512,768]{3,2,1,0:T(8,128)(2,1)}, u32[]{:S(2)}, u32[]{:S(2)}) async-start(bf16[4,4,512,768]{3,2,1,0:T(8,128)(2,1)} %stack.2), calls=%async_computation | async-start | bytes 25165824 | tf_op jit(solution)/shard_map/all_to_all | solution.py:15
  154.4 38.3 %all-to-all-start.3 = ((bf16[64,8,768]{2,1,0:T(8,128)(2,1)}), bf16[64,8,768]{2,1,0:T(8,128)(2,1)S(1)}, u32[]{:S(2)}, u32[]{:S(2)}) async-start(bf16[64,8,768]{2,1,0:T(8,128)(2,1)} %gather_fusion.3), calls=%async_computation.3 | async-start | bytes 1572864 | tf_op jit(solution)/shard_map/all_to_all | solution.py:78
  192.7 28.9 %all-to-all-start.1 = ((bf16[64,8,768]{2,1,0:T(8,128)(2,1)}), bf16[64,8,768]{2,1,0:T(8,128)(2,1)S(1)}, u32[]{:S(2)}, u32[]{:S(2)}) async-start(bf16[64,8,768]{2,1,0:T(8,128)(2,1)} %gather_fusion.1), calls=%async_computation.1 | async-start | bytes 1572864 | tf_op jit(solution)/shard_map/all_to_all | solution.py:78
  221.6 33.3 %all-to-all-start.4 = ((f32[64,1,8]{2,1,0:T(1,128)}), f32[64,1,8]{2,1,0:T(1,128)S(1)}, u32[]{:S(2)}, u32[]{:S(2)}) async-start(f32[64,1,8]{2,1,0:T(1,128)} %bitcast.20), calls=%async_computation.4 | async-start | bytes 65536 | tf_op jit(solution)/shard_map/all_to_all | solution.py:85
  254.9 23.5 %all-to-all-start.2 = ((f32[64,1,8]{2,1,0:T(1,128)}), f32[64,1,8]{2,1,0:T(1,128)S(1)}, u32[]{:S(2)}, u32[]{:S(2)}) async-start(f32[64,1,8]{2,1,0:T(1,128)} %bitcast.10), calls=%async_computation.2 | async-start | bytes 65536 | tf_op jit(solution)/shard_map/all_to_all | solution.py:85
